TPU v7x, 32 devices: a whole 2x2x4 slice. The times are simulated.
32 devices in a mesh: row: 8 (over y, x, core), col: 4 (over z).
Axes of the slice: x: 2, y: 2, z: 4, core: 2. Of those that a mesh axis runs over, the one named last changes fastest.
Arguments:
- pair: bfloat16 [256, 256, 128], P('row', 'col'), may hold values from -6 to 6
- mask: int32 [256], replicated, may hold values 0 or 1
- w_agate: bfloat16 [128, 128], replicated, may hold values from -0.5 to 0.5
- w_aproj: bfloat16 [128, 128], replicated, may hold values from -0.5 to 0.5
- w_bgate: bfloat16 [128, 128], replicated, may hold values from -0.5 to 0.5
- w_bproj: bfloat16 [128, 128], replicated, may hold values from -0.5 to 0.5
- w_gate: bfloat16 [128, 128], replicated, may hold values from -0.5 to 0.5
- w_out: bfloat16 [128, 128], replicated, may hold values from -0.5 to 0.5
- w_up: bfloat16 [128, 512], replicated, may hold values from -0.5 to 0.5
- w_down: bfloat16 [512, 128], replicated, may hold values from -0.25 to 0.25
Outputs:
- updated: bfloat16 [256, 256, 128], P('row', 'col')
All inputs are finite; a program needn't handle non-finite values.
Results may differ from a plain program's by a relative error of at most 0.0059.
Values may be sent and summed in bfloat16 or wider, within the bound.
No kernel may reach another device: no remote copies, remote signals or barrier semaphores. Data moves between devices by JAX's collectives and lax.ppermute only.
A program may use at most 64 MiB of HBM per device.

v0:
```python
import jax
import jax.numpy as jnp
from jax import lax
from jax.sharding import PartitionSpec as P


def layer_norm(values):
    center = values - jnp.mean(values, axis=-1, keepdims=True)
    spread = jnp.mean(center * center, axis=-1, keepdims=True)
    return center * lax.rsqrt(spread + 1e-05)


def body(pair, mask, w_agate, w_aproj, w_bgate, w_bproj, w_gate, w_out, w_up, w_down):
    rows, cols, width = pair.shape
    present = mask.astype(jnp.float32)
    row_start = lax.axis_index("row") * rows
    col_start = lax.axis_index("col") * cols
    row_mask = lax.dynamic_slice_in_dim(present, row_start, rows, 0)
    col_mask = lax.dynamic_slice_in_dim(present, col_start, cols, 0)
    pair_mask = (row_mask[:, None] * col_mask[None, :]).reshape(rows * cols, 1)
    pair_flat = pair.astype(jnp.float32).reshape(rows * cols, width)
    normed = layer_norm(pair_flat).astype(jnp.bfloat16)
    gate = jax.nn.sigmoid(jnp.dot(normed, w_gate, preferred_element_type=jnp.float32))
    left = (
        jax.nn.sigmoid(jnp.dot(normed, w_agate, preferred_element_type=jnp.float32))
        * jnp.dot(normed, w_aproj, preferred_element_type=jnp.float32)
        * pair_mask
    )
    right = (
        jax.nn.sigmoid(jnp.dot(normed, w_bgate, preferred_element_type=jnp.float32))
        * jnp.dot(normed, w_bproj, preferred_element_type=jnp.float32)
        * pair_mask
    )
    left_major = jnp.transpose(left.astype(jnp.bfloat16).reshape(rows, cols, -1), (2, 0, 1))
    right_major = jnp.transpose(right.astype(jnp.bfloat16).reshape(rows, cols, -1), (2, 0, 1))
    left_spread, right_spread = (
        lax.all_to_all(
            lax.all_to_all(left_major, "row", split_axis=0, concat_axis=1, tiled=True),
            "col",
            split_axis=1,
            concat_axis=2,
            tiled=True,
        ),
        lax.all_to_all(
            lax.all_to_all(right_major, "row", split_axis=0, concat_axis=1, tiled=True),
            "col",
            split_axis=1,
            concat_axis=2,
            tiled=True,
        ),
    )
    mixed = jnp.einsum(
        "cik,cjk->cij",
        lax.all_gather(left_spread, "col", axis=1, tiled=True),
        right_spread,
        preferred_element_type=jnp.float32,
    ).astype(jnp.bfloat16)
    mixed = lax.all_to_all(mixed, "row", split_axis=1, concat_axis=0, tiled=True)
    mixed_rows = jnp.transpose(mixed, (1, 2, 0)).astype(jnp.float32).reshape(rows * cols, -1)
    mixed_normed = layer_norm(mixed_rows).astype(jnp.bfloat16)
    middle = pair_flat + gate * jnp.dot(mixed_normed, w_out, preferred_element_type=jnp.float32)
    trans_in = layer_norm(middle).astype(jnp.bfloat16)
    trans_hidden = jax.nn.relu(jnp.dot(trans_in, w_up, preferred_element_type=jnp.float32)).astype(
        jnp.bfloat16
    )
    result = middle + jnp.dot(trans_hidden, w_down, preferred_element_type=jnp.float32)
    return result.astype(jnp.bfloat16).reshape(rows, cols, width)


def solution(mesh):
    placed = (P("row", "col", None), P(), P(), P(), P(), P(), P(), P(), P(), P())
    return jax.shard_map(
        body, mesh=mesh, in_specs=placed, out_specs=P("row", "col", None), check_vma=False
    )
```

profile of v0, /device:TPU:0, one launch (start us, length us, event | category | flops | bytes accessed | tf_op | source)
XLA Modules:
  0.0 144.5 jit_solution(13755586689063979857)
XLA Ops:
  6.5 1.4 convert_reduce_fusion
  8.0 1.7 %multiply_reduce_fusion.2 = f32[32,64]{1,0:T(8,128)S(1)} fusion(bf16[32,64,128]{2,1,0:T(8,128)(2,1)} %param.10, f32[32,64]{1,0:T(8,128)S(1)} %broadcast_multiply_fusion.2), kind=kLoop, calls=%fused_computation.36 | loop fusion | flops 1046528 | bytes 540672 | tf_op jit(solution)/shard_map/reduce_sum | solution.py:9
  9.7 0.7 convert_element_type.47
  10.8 1.6 %fusion.18 = bf16[2048,128]{1,0:T(8,128)(2,1)S(1)} fusion(bf16[32,64,128]{2,1,0:T(8,128)(2,1)} %param.10, f32[2048]{0:T(1024)S(1)} %rsqrt.31, f32[2048]{0:T(1024)S(1)} %div.32), kind=kLoop, calls=%fused_computation.33 | loop fusion | flops 1048576 | bytes 1064960 | tf_op jit(solution)/shard_map/convert_element_type | solution.py:22
  12.5 0.4 fusion.8
  12.9 0.3 copy-done.3
  13.2 0.4 fusion.12
  13.6 1.6 %copy.22 = bf16[32,64,128]{1,0,2:T(8,128)(2,1)S(1)} copy(bf16[32,64,128]{2,1,0:T(8,128)(2,1)S(1)} %bitcast.89) | data formatting | bytes 1048576 | tf_op jit(solution)/shard_map/reshape | solution.py:34
  15.2 0.7 reshape.119
  15.9 14.7 %all_to_all.81 = bf16[8,2,16384]{2,1,0:T(2,128)(2,1)S(1)} all-to-all(bf16[8,2,16384]{2,1,0:T(2,128)(2,1)S(1)} %reshape.119), channel_id=1, replica_groups=mesh['row'=8,'col'=4] {'row'}, dimensions={0} | all-to-all | bytes 1048576 | tf_op jit(solution)/shard_map/all_to_all | solution.py:38
  30.7 0.7 reshape.120
  31.4 0.7 copy.47
  32.1 0.9 reshape.121
  33.0 18.5 %all_to_all.82 = bf16[4,2,32768]{2,1,0:T(2,128)(2,1)S(1)} all-to-all(bf16[4,2,32768]{2,1,0:T(2,128)(2,1)S(1)} %reshape.121), channel_id=1, replica_groups=mesh['row'=8,'col'=4] {'col'}, dimensions={0} | all-to-all | bytes 1048576 | tf_op jit(solution)/shard_map/all_to_all | solution.py:37
  51.5 0.7 reshape.122
  52.2 0.8 copy.45
  53.0 1.5 %all_to_all.66 = bf16[16,64,256]{2,1,0:T(8,128)(2,1)} reshape(bf16[16,64,4,64]{3,2,1,0:T(4,128)(2,1)S(1)} %bitcast.81) | data formatting | bytes 1048576 | tf_op jit(solution)/shard_map/all_to_all | solution.py:37
  54.6 0.4 fusion.4
  55.0 0.3 copy-done.4
  55.3 0.4 fusion.13
  55.7 1.6 %copy.27 = bf16[32,64,128]{1,0,2:T(8,128)(2,1)S(1)} copy(bf16[32,64,128]{2,1,0:T(8,128)(2,1)S(1)} %bitcast.88) | data formatting | bytes 1048576 | tf_op jit(solution)/shard_map/reshape | solution.py:35
  57.3 0.7 reshape.123
  58.0 12.2 %all_to_all.83 = bf16[8,2,16384]{2,1,0:T(2,128)(2,1)S(1)} all-to-all(bf16[8,2,16384]{2,1,0:T(2,128)(2,1)S(1)} %reshape.123), channel_id=1, replica_groups=mesh['row'=8,'col'=4] {'row'}, dimensions={0} | all-to-all | bytes 1048576 | tf_op jit(solution)/shard_map/all_to_all | solution.py:45
  70.2 0.7 reshape.124
  70.9 0.7 copy.46
  71.6 0.9 reshape.125
  72.5 31.4 %all_to_all.84 = bf16[4,2,32768]{2,1,0:T(2,128)(2,1)S(1)} all-to-all(bf16[4,2,32768]{2,1,0:T(2,128)(2,1)S(1)} %reshape.125), channel_id=1, replica_groups=mesh['row'=8,'col'=4] {'col'}, dimensions={0} | all-to-all | bytes 1048576 | tf_op jit(solution)/shard_map/all_to_all | solution.py:44
  103.9 0.7 reshape.126
  104.6 0.8 copy.44
  105.4 0.7 all_to_all.74
  106.1 3.6 %all-gather.2.cloned.1.call-done = bf16[16,256,256]{2,1,0:T(8,128)(2,1)} async-done(((bf16[16,64,256]{2,1,0:T(8,128)(2,1)}), bf16[16,256,256]{2,1,0:T(8,128)(2,1)}) %all-gather.2.cloned.1.call-update) | async-done | bytes 2097168 | tf_op jit(solution)/shard_map/all_gather | solution.py:54
  109.7 2.3 %convolution_convert_fusion = bf16[16,256,64]{1,2,0:T(8,128)(2,1)S(1)} fusion(bf16[16,256,256]{2,1,0:T(8,128)(2,1)} %all-gather.2.cloned.1.call-done, bf16[16,64,256]{2,1,0:T(8,128)(2,1)S(1)} %all_to_all.74), kind=kOutput, calls=%fused_computation.25 | convolution fusion | flops 134479872 | bytes 3145728 | tf_op jit(solution)/shard_map/cik,cjk->cij/dot_general | solution.py:52
  112.0 1.0 copy.32
  113.0 1.5 %reshape.127 = bf16[8,2,16384]{2,1,0:T(2,128)(2,1)} reshape(bf16[256,16,64]{2,1,0:T(8,128)(2,1)S(1)} %bitcast.76) | data formatting | bytes 1048576
  114.5 3.7 %all-to-all-start.4 = ((bf16[8,2,16384]{2,1,0:T(2,128)(2,1)}), bf16[8,2,16384]{2,1,0:T(2,128)(2,1)S(1)}, u32[]{:S(2)}, u32[]{:S(2)}) async-start(bf16[8,2,16384]{2,1,0:T(2,128)(2,1)} %reshape.127), calls=%async_computation.4 | async-start | bytes 1048576 | tf_op jit(solution)/shard_map/all_to_all | solution.py:58
  118.2 1.4 fusion.11
  119.6 8.3 %all-to-all-done.4 = bf16[8,2,16384]{2,1,0:T(2,128)(2,1)S(1)} async-done(((bf16[8,2,16384]{2,1,0:T(2,128)(2,1)}), bf16[8,2,16384]{2,1,0:T(2,128)(2,1)S(1)}, u32[]{:S(2)}, u32[]{:S(2)}) %all-to-all-start.4) | async-done | bytes 524320 | tf_op jit(solution)/shard_map/all_to_all | solution.py:58
  127.9 0.7 reshape.128
  128.6 0.3 copy.33
  128.8 0.3 convert_bitcast_fusion
  129.1 0.2 copy.34
  129.4 0.2 bitcast_reduce_fusion
  129.6 0.3 multiply_reduce_fusion
  130.1 2.3 %copy.35 = f32[32,64,128]{2,1,0:T(8,128)} copy(f32[32,64,128]{1,0,2:T(8,128)S(1)} %bitcast.71) | data formatting | bytes 2097152 | tf_op jit(solution)/shard_map/convert_element_type | solution.py:59
  132.4 1.9 %fusion.16 = bf16[2048,128]{1,0:T(8,128)(2,1)S(1)} fusion(f32[32,64,128]{2,1,0:T(8,128)} %copy.35, f32[2048]{0:T(1024)S(1)} %rsqrt.33, f32[2048]{0:T(1024)S(1)} %div.38), kind=kLoop, calls=%fused_computation.28 | loop fusion | flops 786432 | bytes 1589248 | tf_op jit(solution)/shard_map/convert_element_type | solution.py:60
  134.4 0.5 fusion.24
  134.9 0.6 multiply_reduce_fusion.1
  135.5 2.1 %fusion.14 = bf16[2048,128]{1,0:T(8,128)(2,1)} fusion(f32[2048,128]{1,0:T(8,128)S(1)} %get-tuple-element.6, bf16[512,128]{1,0:T(8,128)(2,1)S(1)} %copy-done, bf16[128,512]{1,0:T(8,128)(2,1)S(1)} %copy-done.6, f32[2048]{0:T(1024)S(1)} %add_rsqrt_fusion.2, f32[2048]{0:T(1024)S(1)} %broadcast_multiply_fusion.3), kind=kOutput, calls=%fused_computation.22 | convolution fusion | flops 540278784 | bytes 1851392 | tf_op jit(solution)/shard_map/dot_general | solution.py:66
  (36 shorter events, 0.9 us)
Async XLA Ops:
  6.5 129.0 %copy-start = (bf16[512,128]{1,0:T(8,128)(2,1)S(1)}, bf16[512,128]{1,0:T(8,128)(2,1)}, u32[]{:S(2)}) copy-start(bf16[512,128]{1,0:T(8,128)(2,1)} %param.19) | copy-start | bytes 393220
  6.5 5.9 %copy-start.7 = (bf16[128,128]{1,0:T(8,128)(2,1)S(1)}, bf16[128,128]{1,0:T(8,128)(2,1)}, u32[]{:S(2)}) copy-start(bf16[128,128]{1,0:T(8,128)(2,1)} %param.12) | copy-start | bytes 98308
  6.5 103.1 %all-gather.2.cloned.1.call-start = ((), (), s32[]{:S(2)}) async-start(), calls=%async_computation.5 | async-start | bytes 2621440 | tf_op jit(solution)/shard_map/all_gather | solution.py:54
  12.5 0.8 copy-start.3
  52.2 2.3 %copy-start.8 = (bf16[128,128]{1,0:T(8,128)(2,1)S(1)}, bf16[128,128]{1,0:T(8,128)(2,1)}, u32[]{:S(2)}) copy-start(bf16[128,128]{1,0:T(8,128)(2,1)} %param.14) | copy-start | bytes 98308
  54.5 0.8 copy-start.4
  112.0 6.2 %copy-start.9 = (bf16[128,128]{1,0:T(8,128)(2,1)S(1)}, bf16[128,128]{1,0:T(8,128)(2,1)}, u32[]{:S(2)}) copy-start(bf16[128,128]{1,0:T(8,128)(2,1)} %param.16) | copy-start | bytes 98308
  114.5 13.4 %all-to-all-start.4 = ((bf16[8,2,16384]{2,1,0:T(2,128)(2,1)}), bf16[8,2,16384]{2,1,0:T(2,128)(2,1)S(1)}, u32[]{:S(2)}, u32[]{:S(2)}) async-start(bf16[8,2,16384]{2,1,0:T(2,128)(2,1)} %reshape.127), calls=%async_computation.4 | async-start | bytes 1048576 | tf_op jit(solution)/shard_map/all_to_all | solution.py:58
  130.0 4.3 %copy-start.1 = (bf16[32,64,128]{2,1,0:T(8,128)(2,1)S(1)}, bf16[32,64,128]{2,1,0:T(8,128)(2,1)}, u32[]{:S(2)}) copy-start(bf16[32,64,128]{2,1,0:T(8,128)(2,1)} %param.10) | copy-start | bytes 1572868
  130.1 4.3 %copy-start.5 = (bf16[128,128]{1,0:T(8,128)(2,1)S(1)}, bf16[128,128]{1,0:T(8,128)(2,1)}, u32[]{:S(2)}) copy-start(bf16[128,128]{1,0:T(8,128)(2,1)} %param.17) | copy-start | bytes 98308
  132.4 1.9 %copy-start.2 = (f32[2048,128]{1,0:T(8,128)S(1)}, f32[2048,128]{1,0:T(8,128)}, u32[]{:S(2)}) copy-start(f32[2048,128]{1,0:T(8,128)} %fusion.11) | copy-start | bytes 3145732
  134.3 1.2 copy-start.6
Sparse Core Ops, SparseCore 0:
  54.6 54.9 all-gather.1
where the time goes:
time: 145 us
  blocking collectives  76.8 us (53%)
  local copies, waits for them, and re-layouts  21.5 us (15%)
  between operations  13.7 us (9%)
  waiting for transfers between devices  11.9 us (8%)
  other arithmetic  8.91 us (6%)
  matrix products  7.95 us (5%)
  starting transfers between devices  3.69 us (3%)
    all_to_all x1, blocking collectives, body(): lax.all_to_all(lax.all_to_all(right_major, 'row', split_axis=0, concat_ax...  31.4 us
    all_to_all x1, blocking collectives, body(): lax.all_to_all(lax.all_to_all(left_major, 'row', split_axis=0, concat_axi...  18.5 us
    all_to_all x1, blocking collectives, body(): lax.all_to_all(left_major, 'row', split_axis=0, concat_axis=1, tiled=True)  14.7 us
    all_to_all x1, blocking collectives, body(): lax.all_to_all(right_major, 'row', split_axis=0, concat_axis=1, tiled=True)  12.2 us
    unnamed x30, local copies, waits for them, and re-layouts  8.68 us
    all_to_all x1, waiting for transfers between devices, body(): lax.all_to_all(mixed, 'row', split_axis=1, concat_axis=0, tiled=True)  8.32 us
    all_to_all x1, starting transfers between devices, body(): lax.all_to_all(mixed, 'row', split_axis=1, concat_axis=0, tiled=True)  3.69 us
    all_gather x1, waiting for transfers between devices, body(): lax.all_gather(left_spread, 'col', axis=1, tiled=True)  3.59 us
  transfers between devices with their start and end apart: 2, of which 2 were waited for; matrix products, arithmetic and copies ran while one was open for 6% of the time, Pallas kernels for 0%

commit v1 on v0

--- a/solution.py
+++ b/solution.py
@@ -2,6 +2,18 @@
 import jax.numpy as jnp
 from jax import lax
 from jax.sharding import PartitionSpec as P
+
+
+def doubled_up(shard, axis, dim):
+    ways, here = (lax.axis_size(axis), lax.axis_index(axis))
+    grown, reach = (shard, 1)
+    while reach < ways:
+        theirs = lax.ppermute(grown, axis, [(d, d ^ reach) for d in range(ways)])
+        mine_first = jnp.concatenate([grown, theirs], axis=dim)
+        theirs_first = jnp.concatenate([theirs, grown], axis=dim)
+        grown = jnp.where(here & reach == 0, mine_first, theirs_first)
+        reach = 2 * reach
+    return grown
 
 
 def layer_norm(values):
@@ -51,7 +63,7 @@
     )
     mixed = jnp.einsum(
         "cik,cjk->cij",
-        lax.all_gather(left_spread, "col", axis=1, tiled=True),
+        doubled_up(left_spread, "col", 1),
         right_spread,
         preferred_element_type=jnp.float32,
     ).astype(jnp.bfloat16)

time: 145 us -> 150 us (1.034)
  waiting for transfers between devices: 11.9 us -> 62.6 us
  blocking collectives: 76.8 us -> 33.2 us
  between operations: 13.7 us -> 0.39 us
  starting transfers between devices: 3.69 us -> 12.2 us
    all_to_all x0 -> x2, waiting for transfers between devices: none -> 50 us  [the longest x1 47.4 us: body(): lax.all_to_all(lax.all_to_all(right_major, 'row', split_axis=0, concat_ax...]
    all_to_all x2 -> x0, blocking collectives: 43.5 us -> none  [the longest x1 31.4 us: body(): lax.all_to_all(lax.all_to_all(right_major, 'row', split_axis=0, concat_ax...]
    all_to_all x0 -> x2, starting transfers between devices: none -> 7.15 us  [the longest x1 3.67 us: body(): lax.all_to_all(right_major, 'row', split_axis=0, concat_axis=1, tiled=True)]
    ppermute x0 -> x2, waiting for transfers between devices: none -> 4.57 us  [doubled_up(): theirs = lax.ppermute(grown, axis, [(d, d ^ reach) for d in range(ways)])]
    all_gather x1 -> x0, waiting for transfers between devices: 3.59 us -> none  [body(): lax.all_gather(left_spread, 'col', axis=1, tiled=True)]
  transfers between devices with their start and end apart: 2 -> 5, of which waited for: 2 -> 4; matrix products, arithmetic and copies ran while one was open for 6% -> 7% of each run, Pallas kernels for 0% -> 0%
where the time goes in v1:
time: 150 us; the launch traced here: 149 us
  waiting for transfers between devices  62.6 us (42%)
  blocking collectives  33.2 us (22%)
  local copies, waits for them, and re-layouts  22 us (15%)
  starting transfers between devices  12.2 us (8%)
  other arithmetic  10.2 us (7%)
  matrix products  8.62 us (6%)
    all_to_all x1, waiting for transfers between devices, body(): lax.all_to_all(lax.all_to_all(right_major, 'row', split_axis=0, concat_ax...  47.4 us
    all_to_all x1, blocking collectives, body(): lax.all_to_all(lax.all_to_all(left_major, 'row', split_axis=0, concat_axi...  18.5 us
    all_to_all x1, blocking collectives, body(): lax.all_to_all(left_major, 'row', split_axis=0, concat_axis=1, tiled=True)  14.7 us
    unnamed x30, local copies, waits for them, and re-layouts  9.92 us
    all_to_all x1, waiting for transfers between devices, body(): lax.all_to_all(mixed, 'row', split_axis=1, concat_axis=0, tiled=True)  8.04 us
    ppermute x2, waiting for transfers between devices, doubled_up(): theirs = lax.ppermute(grown, axis, [(d, d ^ reach) for d in range(ways)])  4.57 us
    all_to_all x1, starting transfers between devices, body(): lax.all_to_all(mixed, 'row', split_axis=1, concat_axis=0, tiled=True)  3.71 us
    all_to_all x1, starting transfers between devices, body(): lax.all_to_all(right_major, 'row', split_axis=0, concat_axis=1, tiled=True)  3.67 us
  transfers between devices with their start and end apart: 5, of which 4 were waited for; matrix products, arithmetic and copies ran while one was open for 7% of the time, Pallas kernels for 0%

profile of v1, /device:TPU:0, one launch (start us, length us, event | category | flops | bytes accessed | tf_op | source)
XLA Modules:
  0.0 149.2 jit_solution(4402716232668607041)
XLA Ops:
  0.0 1.4 convert_reduce_fusion
  1.4 1.7 %multiply_reduce_fusion.2 = f32[32,64]{1,0:T(8,128)S(1)} fusion(bf16[32,64,128]{2,1,0:T(8,128)(2,1)} %param.10, f32[32,64]{1,0:T(8,128)S(1)} %broadcast_multiply_fusion.2), kind=kLoop, calls=%fused_computation.45 | loop fusion | flops 1046528 | bytes 540672 | tf_op jit(solution)/shard_map/reduce_sum | solution.py:21
  3.2 0.7 convert_element_type.47
  4.3 1.6 %fusion.26 = bf16[2048,128]{1,0:T(8,128)(2,1)S(1)} fusion(bf16[32,64,128]{2,1,0:T(8,128)(2,1)} %param.10, f32[2048]{0:T(1024)S(1)} %rsqrt.31, f32[2048]{0:T(1024)S(1)} %div.32), kind=kLoop, calls=%fused_computation.42 | loop fusion | flops 1048576 | bytes 1064960 | tf_op jit(solution)/shard_map/convert_element_type | solution.py:34
  5.9 0.4 fusion.8
  6.4 0.3 copy-done.3
  6.7 0.4 fusion.12
  7.1 1.6 %copy.32 = bf16[32,64,128]{1,0,2:T(8,128)(2,1)S(1)} copy(bf16[32,64,128]{2,1,0:T(8,128)(2,1)S(1)} %bitcast.88) | data formatting | bytes 1048576 | tf_op jit(solution)/shard_map/reshape | solution.py:46
  8.7 0.7 reshape.123
  9.4 14.7 %all_to_all.81 = bf16[8,2,16384]{2,1,0:T(2,128)(2,1)S(1)} all-to-all(bf16[8,2,16384]{2,1,0:T(2,128)(2,1)S(1)} %reshape.123), channel_id=1, replica_groups=mesh['row'=8,'col'=4] {'row'}, dimensions={0} | all-to-all | bytes 1048576 | tf_op jit(solution)/shard_map/all_to_all | solution.py:50
  24.1 0.7 reshape.124
  24.9 0.7 copy.57
  25.6 0.9 reshape.125
  26.4 18.5 %all_to_all.82 = bf16[4,2,32768]{2,1,0:T(2,128)(2,1)S(1)} all-to-all(bf16[4,2,32768]{2,1,0:T(2,128)(2,1)S(1)} %reshape.125), channel_id=1, replica_groups=mesh['row'=8,'col'=4] {'col'}, dimensions={0} | all-to-all | bytes 1048576 | tf_op jit(solution)/shard_map/all_to_all | solution.py:49
  44.9 0.7 reshape.126
  45.7 0.8 copy.55
  46.5 0.7 all_to_all.66
  47.2 0.3 collective-permute-start
  47.5 0.4 fusion.4
  47.9 0.4 fusion.13
  48.3 1.6 %copy.37 = bf16[32,64,128]{1,0,2:T(8,128)(2,1)S(1)} copy(bf16[32,64,128]{2,1,0:T(8,128)(2,1)S(1)} %bitcast.87) | data formatting | bytes 1048576 | tf_op jit(solution)/shard_map/reshape | solution.py:47
  49.9 1.5 %reshape.119 = bf16[8,2,16384]{2,1,0:T(2,128)(2,1)} reshape(bf16[128,32,64]{2,1,0:T(8,128)(2,1)S(1)} %bitcast.74) | data formatting | bytes 1048576
  51.4 3.7 %all-to-all-start.2 = ((bf16[8,2,16384]{2,1,0:T(2,128)(2,1)}), bf16[8,2,16384]{2,1,0:T(2,128)(2,1)S(1)}, u32[]{:S(2)}, u32[]{:S(2)}) async-start(bf16[8,2,16384]{2,1,0:T(2,128)(2,1)} %reshape.119), calls=%async_computation.2 | async-start | bytes 1048576 | tf_op jit(solution)/shard_map/all_to_all | solution.py:57
  55.1 4.6 %collective-permute-done = bf16[16,64,256]{2,1,0:T(8,128)(2,1)S(1)} collective-permute-done((bf16[16,64,256]{2,1,0:T(8,128)(2,1)S(1)}, bf16[16,64,256]{2,1,0:T(8,128)(2,1)S(1)}, u32[]{:S(2)}, u32[]{:S(2)}) %collective-permute-start) | collective-permute-done | bytes 524320 | tf_op jit(solution)/shard_map/ppermute | solution.py:11
  59.7 1.3 maximum_select_fusion.4
  61.0 1.0 collective-permute-start.1
  62.0 2.6 %all-to-all-done.2 = bf16[8,2,16384]{2,1,0:T(2,128)(2,1)S(1)} async-done(((bf16[8,2,16384]{2,1,0:T(2,128)(2,1)}), bf16[8,2,16384]{2,1,0:T(2,128)(2,1)S(1)}, u32[]{:S(2)}, u32[]{:S(2)}) %all-to-all-start.2) | async-done | bytes 524320 | tf_op jit(solution)/shard_map/all_to_all | solution.py:57
  64.6 0.7 reshape.120
  65.4 0.7 copy.56
  66.1 1.6 %reshape.121 = bf16[4,2,32768]{2,1,0:T(2,128)(2,1)} reshape(bf16[256,16,64]{2,1,0:T(8,128)(2,1)S(1)} %bitcast.83) | data formatting | bytes 1048576
  67.6 3.5 %all-to-all-start.3 = ((bf16[4,2,32768]{2,1,0:T(2,128)(2,1)}), bf16[4,2,32768]{2,1,0:T(2,128)(2,1)S(1)}, u32[]{:S(2)}, u32[]{:S(2)}) async-start(bf16[4,2,32768]{2,1,0:T(2,128)(2,1)} %reshape.121), calls=%async_computation.3 | async-start | bytes 1048576 | tf_op jit(solution)/shard_map/all_to_all | solution.py:56
  71.1 47.4 %all-to-all-done.3 = bf16[4,2,32768]{2,1,0:T(2,128)(2,1)S(1)} async-done(((bf16[4,2,32768]{2,1,0:T(2,128)(2,1)}), bf16[4,2,32768]{2,1,0:T(2,128)(2,1)S(1)}, u32[]{:S(2)}, u32[]{:S(2)}) %all-to-all-start.3) | async-done | bytes 524320 | tf_op jit(solution)/shard_map/all_to_all | solution.py:56
  118.6 0.7 reshape.122
  119.3 0.8 copy.54
  120.1 0.7 all_to_all.74
  120.8 3.0 %fusion.22 = bf16[16,256,64]{1,2,0:T(8,128)(2,1)S(1)} fusion(bf16[16,64,256]{2,1,0:T(8,128)(2,1)S(1)} %all_to_all.74, bf16[16,128,256]{2,1,0:T(8,128)(2,1)} %collective-permute-done.1, bf16[16,128,256]{2,1,0:T(8,128)(2,1)} %maximum_select_fusion.4, pred[]{:T(512)S(6)} %eq.6), kind=kOutput, calls=%fused_computation.33 | convolution fusion | flops 143917056 | bytes 3145729 | tf_op jit(solution)/shard_map/cik,cjk->cij/dot_general | solution.py:64
  123.8 1.0 copy.42
  124.8 1.5 %reshape.127 = bf16[8,2,16384]{2,1,0:T(2,128)(2,1)} reshape(bf16[256,16,64]{2,1,0:T(8,128)(2,1)S(1)} %bitcast.75) | data formatting | bytes 1048576
  126.3 3.7 %all-to-all-start.4 = ((bf16[8,2,16384]{2,1,0:T(2,128)(2,1)}), bf16[8,2,16384]{2,1,0:T(2,128)(2,1)S(1)}, u32[]{:S(2)}, u32[]{:S(2)}) async-start(bf16[8,2,16384]{2,1,0:T(2,128)(2,1)} %reshape.127), calls=%async_computation.4 | async-start | bytes 1048576 | tf_op jit(solution)/shard_map/all_to_all | solution.py:70
  130.0 1.4 fusion.11
  131.4 8.0 %all-to-all-done.4 = bf16[8,2,16384]{2,1,0:T(2,128)(2,1)S(1)} async-done(((bf16[8,2,16384]{2,1,0:T(2,128)(2,1)}), bf16[8,2,16384]{2,1,0:T(2,128)(2,1)S(1)}, u32[]{:S(2)}, u32[]{:S(2)}) %all-to-all-start.4) | async-done | bytes 524320 | tf_op jit(solution)/shard_map/all_to_all | solution.py:70
  139.5 0.7 reshape.128
  141.1 0.3 multiply_reduce_fusion
  141.6 2.3 %copy.45 = f32[32,64,128]{2,1,0:T(8,128)} copy(f32[32,64,128]{1,0,2:T(8,128)S(1)} %bitcast.70) | data formatting | bytes 2097152 | tf_op jit(solution)/shard_map/convert_element_type | solution.py:71
  144.0 1.9 %fusion.24 = bf16[2048,128]{1,0:T(8,128)(2,1)S(1)} fusion(f32[32,64,128]{2,1,0:T(8,128)} %copy.45, f32[2048]{0:T(1024)S(1)} %rsqrt.33, f32[2048]{0:T(1024)S(1)} %div.38), kind=kLoop, calls=%fused_computation.37 | loop fusion | flops 786432 | bytes 1589248 | tf_op jit(solution)/shard_map/convert_element_type | solution.py:72
  145.9 0.5 fusion.33
  146.4 0.6 multiply_reduce_fusion.1
  147.1 2.1 %fusion.14 = bf16[2048,128]{1,0:T(8,128)(2,1)} fusion(f32[2048,128]{1,0:T(8,128)S(1)} %get-tuple-element.6, bf16[512,128]{1,0:T(8,128)(2,1)S(1)} %copy-done, bf16[128,512]{1,0:T(8,128)(2,1)S(1)} %copy-done.6, f32[2048]{0:T(1024)S(1)} %add_rsqrt_fusion.2, f32[2048]{0:T(1024)S(1)} %broadcast_multiply_fusion.3), kind=kOutput, calls=%fused_computation.22 | convolution fusion | flops 540278784 | bytes 1851392 | tf_op jit(solution)/shard_map/dot_general | solution.py:78
  (40 shorter events, 1.9 us)
Async XLA Ops:
  0.0 147.1 %copy-start = (bf16[512,128]{1,0:T(8,128)(2,1)S(1)}, bf16[512,128]{1,0:T(8,128)(2,1)}, u32[]{:S(2)}) copy-start(bf16[512,128]{1,0:T(8,128)(2,1)} %param.19) | copy-start | bytes 393220
  0.0 5.9 %copy-start.7 = (bf16[128,128]{1,0:T(8,128)(2,1)S(1)}, bf16[128,128]{1,0:T(8,128)(2,1)}, u32[]{:S(2)}) copy-start(bf16[128,128]{1,0:T(8,128)(2,1)} %param.12) | copy-start | bytes 98308
  5.9 0.8 copy-start.3
  45.7 1.8 %copy-start.8 = (bf16[128,128]{1,0:T(8,128)(2,1)S(1)}, bf16[128,128]{1,0:T(8,128)(2,1)}, u32[]{:S(2)}) copy-start(bf16[128,128]{1,0:T(8,128)(2,1)} %param.14) | copy-start | bytes 98308
  47.2 0.8 copy-start.4
  47.2 12.5 %collective-permute-start = (bf16[16,64,256]{2,1,0:T(8,128)(2,1)S(1)}, bf16[16,64,256]{2,1,0:T(8,128)(2,1)S(1)}, u32[]{:S(2)}, u32[]{:S(2)}) collective-permute-start(bf16[16,64,256]{2,1,0:T(8,128)(2,1)S(1)} %all_to_all.66), channel_id=1, source_target_pairs={{0,1},{1,0},{2,3},{3,2},{4,5},{5,4},{6,7},{7,6},{8,9},{9,8},{10,11... | collective-permute-start | bytes 1572872 | tf_op jit(solution)/shard_map/ppermute | solution.py:11
  51.4 13.2 %all-to-all-start.2 = ((bf16[8,2,16384]{2,1,0:T(2,128)(2,1)}), bf16[8,2,16384]{2,1,0:T(2,128)(2,1)S(1)}, u32[]{:S(2)}, u32[]{:S(2)}) async-start(bf16[8,2,16384]{2,1,0:T(2,128)(2,1)} %reshape.119), calls=%async_computation.2 | async-start | bytes 1048576 | tf_op jit(solution)/shard_map/all_to_all | solution.py:57
  61.0 59.8 %collective-permute-start.1 = (bf16[16,128,256]{2,1,0:T(8,128)(2,1)}, bf16[16,128,256]{2,1,0:T(8,128)(2,1)}, u32[]{:S(2)}, u32[]{:S(2)}) collective-permute-start(bf16[16,128,256]{2,1,0:T(8,128)(2,1)} %maximum_select_fusion.4), channel_id=1, source_target_pairs={{0,2},{1,3},{2,0},{3,1},{4,6},{5,7},{6,4},{7,5},{8,10},{9,11},{10,... | collective-permute-start | bytes 3145736 | tf_op jit(solution)/shard_map/ppermute | solution.py:11
  67.6 50.9 %all-to-all-start.3 = ((bf16[4,2,32768]{2,1,0:T(2,128)(2,1)}), bf16[4,2,32768]{2,1,0:T(2,128)(2,1)S(1)}, u32[]{:S(2)}, u32[]{:S(2)}) async-start(bf16[4,2,32768]{2,1,0:T(2,128)(2,1)} %reshape.121), calls=%async_computation.3 | async-start | bytes 1048576 | tf_op jit(solution)/shard_map/all_to_all | solution.py:56
  123.8 6.2 %copy-start.9 = (bf16[128,128]{1,0:T(8,128)(2,1)S(1)}, bf16[128,128]{1,0:T(8,128)(2,1)}, u32[]{:S(2)}) copy-start(bf16[128,128]{1,0:T(8,128)(2,1)} %param.16) | copy-start | bytes 98308
  126.3 13.2 %all-to-all-start.4 = ((bf16[8,2,16384]{2,1,0:T(2,128)(2,1)}), bf16[8,2,16384]{2,1,0:T(2,128)(2,1)S(1)}, u32[]{:S(2)}, u32[]{:S(2)}) async-start(bf16[8,2,16384]{2,1,0:T(2,128)(2,1)} %reshape.127), calls=%async_computation.4 | async-start | bytes 1048576 | tf_op jit(solution)/shard_map/all_to_all | solution.py:70
  141.6 4.3 %copy-start.1 = (bf16[32,64,128]{2,1,0:T(8,128)(2,1)S(1)}, bf16[32,64,128]{2,1,0:T(8,128)(2,1)}, u32[]{:S(2)}) copy-start(bf16[32,64,128]{2,1,0:T(8,128)(2,1)} %param.10) | copy-start | bytes 1572868
  141.6 4.3 %copy-start.5 = (bf16[128,128]{1,0:T(8,128)(2,1)S(1)}, bf16[128,128]{1,0:T(8,128)(2,1)}, u32[]{:S(2)}) copy-start(bf16[128,128]{1,0:T(8,128)(2,1)} %param.17) | copy-start | bytes 98308
  144.0 1.9 %copy-start.2 = (f32[2048,128]{1,0:T(8,128)S(1)}, f32[2048,128]{1,0:T(8,128)}, u32[]{:S(2)}) copy-start(f32[2048,128]{1,0:T(8,128)} %fusion.11) | copy-start | bytes 3145732
  145.9 1.2 copy-start.6
